TPU v7x, 32 devices: a whole 2x2x4 slice. The times are simulated.
32 devices in a mesh: groups: 2 (over y), gz: 4 (over z), sec: 2 (over x), ch: 2 (over core).
Axes of the slice: x: 2, y: 2, z: 4, core: 2. Of those that a mesh axis runs over, the one named last changes fastest.
Arguments:
- coarse: bfloat16 [64, 32, 4, 256], P('ch', ('groups', 'gz', 'sec')), parts along dimension 1, may hold values from -6 to 6
- saved_pre: bfloat16 [32, 64, 8, 512], P('ch', ('groups', 'gz', 'sec')), parts along dimension 1, may hold values from -6 to 6
- out_grad: bfloat16 [32, 64, 8, 512], P('ch', ('groups', 'gz', 'sec')), parts along dimension 1, may hold values from -6 to 6
- up_weight: bfloat16 [27, 32, 64], replicated, may hold values from -0.21875 to 0.21875
- refine_weight: bfloat16 [27, 32, 32], replicated, may hold values from -0.21875 to 0.21875
Outputs:
- grad_coarse: bfloat16 [64, 32, 4, 256], P('ch', ('groups', 'gz', 'sec')), parts along dimension 1
- grad_up: float32 [54, 32, 64], P('groups', 'ch'), parts along dimension 0
- grad_refine: float32 [54, 32, 32], P('groups', None, 'ch'), parts along dimension 0
There are 2 independent parts, one for each index of `groups`. A program takes and returns all parts, laid end to end along the dimension named above; an argument that names none is the same for every part. Nothing has to cross between parts.
All inputs are finite; a program needn't handle non-finite values.
Results may differ from a plain program's by a relative error of at most 0.0049.
Values may be sent and summed in bfloat16 or wider, within the bound.
No kernel may reach another device: no remote copies, remote signals or barrier semaphores. Data moves between devices by JAX's collectives and lax.ppermute only.
A program may use at most 128 MiB of HBM per device.

v0:
```python
import jax
import jax.numpy as jnp
from jax import lax
from jax.sharding import PartitionSpec as P

leak_slope = 0.2


def padded(block, sides, width):
    for axis, dim in sides:
        count = lax.axis_size(axis)
        forward = [(i, i + 1) for i in range(count - 1)]
        forward.append((count - 1, 0))
        backward = [(target, source) for source, target in forward]
        low = lax.ppermute(
            lax.slice_in_dim(block, block.shape[dim] - width, None, axis=dim), axis, forward
        )
        high = lax.ppermute(lax.slice_in_dim(block, 0, width, axis=dim), axis, backward)
        block = jnp.concatenate([low, block, high], axis=dim)
    return block


def passed_along(block, axis, distance):
    devices = range(lax.axis_size(axis))
    route = [((i - distance) % len(devices), i) for i in devices]
    return lax.ppermute(block, axis, route)


def kernel_offsets():
    return [
        (along_z, along_x, along_y)
        for along_z in range(3)
        for along_x in range(3)
        for along_y in range(3)
    ]


def take_taps(source, along_z, along_x, along_y, coarse_z, coarse_x):
    selected = source[
        :, along_z : along_z + 2 * coarse_z : 2, along_x : along_x + 2 * coarse_x : 2, :
    ]
    return jnp.roll(selected, 1 - along_y, axis=3)[:, :, :, ::2]


def local(coarse, saved_pre, out_grad, up_weight, refine_weight):
    part_ch = saved_pre.shape[0]
    planes_z = saved_pre.shape[1]
    planes_x = saved_pre.shape[2]
    cells_y = saved_pre.shape[3]
    coarse_z = planes_z // 2
    coarse_x = planes_x // 2
    channel_start = lax.axis_index("ch") * part_ch
    pre_act = saved_pre.astype(jnp.float32)
    slopes = jnp.where(pre_act > 0, 1.0, leak_slope).astype(jnp.float32)
    hidden = (pre_act * slopes).astype(jnp.bfloat16)
    every_channel = lax.all_gather(out_grad, "ch", axis=0, tiled=True)
    rimmed_z = padded(every_channel, ((("gz", "sec"), 1),), 2)
    rimmed = jnp.pad(rimmed_z, ((0, 0), (0, 0), (2, 2), (0, 0)))
    refine_cols = lax.dynamic_slice_in_dim(refine_weight, channel_start, part_ch, 2)
    grad_hidden = jnp.zeros(pre_act.shape, jnp.float32)
    refine_terms = []
    for tap_number, (along_z, along_x, along_y) in enumerate(kernel_offsets()):
        shifted = rimmed[
            :,
            4 - 2 * along_z : 4 - 2 * along_z + planes_z,
            4 - 2 * along_x : 4 - 2 * along_x + planes_x,
            :,
        ]
        shifted = jnp.roll(shifted, 2 * (along_y - 1), axis=3)
        grad_hidden = grad_hidden + jnp.einsum(
            "oc,ozxy->czxy", refine_cols[tap_number], shifted, preferred_element_type=jnp.float32
        )
        refine_terms.append(
            jnp.einsum("ozxy,czxy->oc", shifted, hidden, preferred_element_type=jnp.float32)
        )
    grad_pre = (grad_hidden * slopes).astype(jnp.bfloat16)
    below_z = passed_along(grad_pre[:, planes_z - 1 :, :, :], ("gz", "sec"), 1)
    raised_z = jnp.concatenate([below_z, grad_pre], axis=1)
    extended = jnp.pad(raised_z, ((0, 0), (0, 0), (1, 0), (0, 0)))
    selections = [
        take_taps(extended, along_z, along_x, along_y, coarse_z, coarse_x)
        for along_z, along_x, along_y in kernel_offsets()
    ]
    all_coarse = lax.all_gather(coarse, "ch", axis=0, tiled=True)
    up_terms = [
        jnp.einsum("czxy,fzxy->fc", all_coarse, selected, preferred_element_type=jnp.float32)
        for selected in selections
    ]
    up_rows = lax.dynamic_slice_in_dim(up_weight, channel_start, part_ch, 1)
    running = jnp.zeros((coarse.shape[0] * lax.axis_size("ch"),) + coarse.shape[1:], jnp.float32)
    for tap_number, selected in enumerate(selections):
        weight_block = up_rows[tap_number]
        running = running + jnp.einsum(
            "fc,fzxy->czxy", weight_block, selected, preferred_element_type=jnp.float32
        )
    coarse_summed = lax.psum_scatter(running, "ch", scatter_dimension=0, tiled=True)
    grad_coarse = coarse_summed.astype(jnp.bfloat16)
    up_summed, refine_summed = lax.psum(
        (jnp.stack(up_terms), jnp.stack(refine_terms)), ("gz", "sec")
    )
    fine_total = planes_z * lax.axis_size("gz") * lax.axis_size("sec") * planes_x * cells_y
    coarse_total = fine_total // 8
    grad_up = up_summed * float(coarse_total) ** (-0.5)
    grad_refine = refine_summed * float(fine_total) ** (-0.5)
    return (grad_coarse, grad_up, grad_refine)


def solution(mesh):
    placed = (
        P("ch", ("groups", "gz", "sec"), None, None),
        P("ch", ("groups", "gz", "sec"), None, None),
        P("ch", ("groups", "gz", "sec"), None, None),
        P(),
        P(),
    )
    return jax.shard_map(
        local,
        mesh=mesh,
        in_specs=placed,
        out_specs=(
            P("ch", ("groups", "gz", "sec"), None, None),
            P("groups", "ch", None),
            P("groups", None, "ch"),
        ),
        check_vma=False,
    )
```

profile of v0, /device:TPU:0, one launch (start us, length us, event | category | flops | bytes accessed | tf_op | source)
XLA Modules:
  0.0 347.9 jit_solution(7144376566447000384)
XLA Ops:
  12.5 8.8 %all-gather.2.cloned.1.call-done = bf16[32,4,8,512]{3,0,2,1:T(8,128)(2,1)} async-done(((bf16[16,4,8,512]{3,0,2,1:T(8,128)(2,1)}), bf16[32,4,8,512]{3,0,2,1:T(8,128)(2,1)}) %all-gather.2.cloned.1.call-update) | async-done | bytes 1048592 | tf_op jit(solution)/shard_map/all_gather | solution.py:56
  24.5 3.0 collective-permute-start.1
  29.0 18.3 %collective-permute-done = bf16[32,2,8,512]{3,0,2,1:T(8,128)(2,1)S(1)} collective-permute-done((bf16[32,2,8,512]{3,0,2,1:T(8,128)(2,1)S(1)}, bf16[32,2,8,512]{3,0,2,1:T(8,128)(2,1)S(1)}, u32[]{:S(2)}, u32[]{:S(2)}) %collective-permute-start) | collective-permute-done | bytes 524320 | tf_op jit(solution)/shard_map/ppermute | solution.py:15
  50.0 4.9 %fusion.280 = (bf16[32,4,8,510]{3,0,2,1:T(8,128)(2,1)S(1)}, bf16[32,4,8,510]{3,0,2,1:T(8,128)(2,1)S(1)}, bf16[32,4,8,510]{3,0,2,1:T(8,128)(2,1)S(1)}, bf16[32,4,...) fusion(bf16[32,8,12,512]{3,0,2,1:T(8,128)(2,1)S(1)} %fusion.5), kind=kLoop, calls=%fused_computation.425 | loop fusion | bytes 25067520 | tf_op jit(solution)/shard_map/jit(_roll_static)/slice | solution.py:69
  100.4 6.5 %collective-permute-done.2 = bf16[16,1,8,512]{3,0,2,1:T(8,128)(2,1)S(1)} collective-permute-done((bf16[16,1,8,512]{3,0,2,1:T(8,128)(2,1)S(1)}, bf16[16,1,8,512]{3,0,2,1:T(8,128)(2,1)S(1)}, u32[]{:S(2)}, u32[]{:S(2)}) %collective-permute-start.2) | collective-permute-done | bytes 131104 | tf_op jit(solution)/shard_map/ppermute | solution.py:26
  109.2 4.1 %slice.685 = bf16[16,2,4,256]{3,0,2,1:T(8,128)(2,1)} slice(bf16[16,2,4,512]{3,0,2,1:T(8,128)(2,1)} %copy-done.2), slice={[0:16:1], [0:2:1], [0:4:1], [0:512:2]} | slice | bytes 131072 | tf_op jit(solution)/shard_map/slice | solution.py:42
  116.6 3.8 %slice.696 = bf16[16,2,4,256]{3,0,2,1:T(8,128)(2,1)} slice(bf16[16,2,4,512]{3,0,2,1:T(8,128)(2,1)} %get-tuple-element.59), slice={[0:16:1], [0:2:1], [0:4:1], [0:512:2]} | slice | bytes 131072 | tf_op jit(solution)/shard_map/slice | solution.py:42
  159.2 3.3 slice.700
  164.2 3.8 %slice.705 = bf16[16,2,4,256]{3,0,2,1:T(8,128)(2,1)} slice(bf16[16,2,4,512]{3,0,2,1:T(8,128)(2,1)} %pad_maximum_fusion.22), slice={[0:16:1], [0:2:1], [0:4:1], [0:512:2]} | slice | bytes 131072 | tf_op jit(solution)/shard_map/slice | solution.py:42
  169.6 3.2 slice.711
  174.5 3.8 %slice.716 = bf16[16,2,4,256]{3,0,2,1:T(8,128)(2,1)} slice(bf16[16,2,4,512]{3,0,2,1:T(8,128)(2,1)} %pad_maximum_fusion.24), slice={[0:16:1], [0:2:1], [0:4:1], [0:512:2]} | slice | bytes 131072 | tf_op jit(solution)/shard_map/slice | solution.py:42
  179.9 3.2 slice.722
  184.7 3.8 %slice.727 = bf16[16,2,4,256]{3,0,2,1:T(8,128)(2,1)} slice(bf16[16,2,4,512]{3,0,2,1:T(8,128)(2,1)} %pad_maximum_fusion.26), slice={[0:16:1], [0:2:1], [0:4:1], [0:512:2]} | slice | bytes 131072 | tf_op jit(solution)/shard_map/slice | solution.py:42
  190.2 3.8 %slice.733 = bf16[16,2,4,256]{3,0,2,1:T(8,128)(2,1)} slice(bf16[16,2,4,512]{3,0,2,1:T(8,128)(2,1)} %pad_maximum_fusion.27), slice={[0:16:1], [0:2:1], [0:4:1], [0:512:2]} | slice | bytes 131072 | tf_op jit(solution)/shard_map/slice | solution.py:42
  195.6 3.8 %slice.738 = bf16[16,2,4,256]{3,0,2,1:T(8,128)(2,1)} slice(bf16[16,2,4,512]{3,0,2,1:T(8,128)(2,1)} %pad_maximum_fusion.28), slice={[0:16:1], [0:2:1], [0:4:1], [0:512:2]} | slice | bytes 131072 | tf_op jit(solution)/shard_map/slice | solution.py:42
  201.0 3.8 %slice.744 = bf16[16,2,4,256]{3,0,2,1:T(8,128)(2,1)} slice(bf16[16,2,4,512]{3,0,2,1:T(8,128)(2,1)} %pad_maximum_fusion.29), slice={[0:16:1], [0:2:1], [0:4:1], [0:512:2]} | slice | bytes 131072 | tf_op jit(solution)/shard_map/slice | solution.py:42
  206.4 3.8 %slice.749 = bf16[16,2,4,256]{3,0,2,1:T(8,128)(2,1)} slice(bf16[16,2,4,512]{3,0,2,1:T(8,128)(2,1)} %pad_maximum_fusion.30), slice={[0:16:1], [0:2:1], [0:4:1], [0:512:2]} | slice | bytes 131072 | tf_op jit(solution)/shard_map/slice | solution.py:42
  211.8 3.8 %slice.755 = bf16[16,2,4,256]{3,0,2,1:T(8,128)(2,1)} slice(bf16[16,2,4,512]{3,0,2,1:T(8,128)(2,1)} %pad_maximum_fusion.31), slice={[0:16:1], [0:2:1], [0:4:1], [0:512:2]} | slice | bytes 131072 | tf_op jit(solution)/shard_map/slice | solution.py:42
  217.3 3.8 %slice.760 = bf16[16,2,4,256]{3,0,2,1:T(8,128)(2,1)} slice(bf16[16,2,4,512]{3,0,2,1:T(8,128)(2,1)} %pad_maximum_fusion.32), slice={[0:16:1], [0:2:1], [0:4:1], [0:512:2]} | slice | bytes 131072 | tf_op jit(solution)/shard_map/slice | solution.py:42
  222.7 3.9 %slice.766 = bf16[16,2,4,256]{3,0,2,1:T(8,128)(2,1)} slice(bf16[16,2,4,512]{3,0,2,1:T(8,128)(2,1)} %pad_maximum_fusion.33), slice={[0:16:1], [0:2:1], [0:4:1], [0:512:2]} | slice | bytes 131072 | tf_op jit(solution)/shard_map/slice | solution.py:42
  228.3 3.8 %slice.771 = bf16[16,2,4,256]{3,0,2,1:T(8,128)(2,1)} slice(bf16[16,2,4,512]{3,0,2,1:T(8,128)(2,1)} %pad_maximum_fusion.34), slice={[0:16:1], [0:2:1], [0:4:1], [0:512:2]} | slice | bytes 131072 | tf_op jit(solution)/shard_map/slice | solution.py:42
  233.7 3.2 slice.777
  292.9 36.5 %psum.15 = f32[27,32,16]{1,2,0:T(8,128)S(1)} all-reduce(f32[27,32,16]{1,2,0:T(8,128)S(1)} %fusion.16), channel_id=1, replica_groups=mesh['groups'=2,'gz'=4,'sec'=2,'ch'=2] {'gz','sec'}, use_global_device_ids=true, to_apply=%region_2.3 | all-reduce | flops 13824 | bytes 110592 | tf_op jit(solution)/shard_map/psum | solution.py:98
  331.8 7.7 %reduce-scatter.2.cloned.1.call-done = f32[32,2,4,256]{3,0,2,1:T(8,128)} async-done(((f32[64,2,4,256]{3,0,2,1:T(8,128)}), f32[32,2,4,256]{3,0,2,1:T(8,128)}) %reduce-scatter.2.cloned.1.call-update) | async-done | bytes 262160 | tf_op jit(solution)/shard_map/reduce_scatter | solution.py:96
  (279 shorter events, 184.9 us)
Async XLA Ops:
  7.2 79.5 %copy-start = (bf16[27,32,32]{2,1,0:T(8,128)(2,1)S(1)}, bf16[27,32,32]{2,1,0:T(8,128)(2,1)}, u32[]{:S(2)}) copy-start(bf16[27,32,32]{2,1,0:T(8,128)(2,1)} %param.9) | copy-start | bytes 165892
  7.2 14.1 %all-gather.2.cloned.1.call-start = ((), (), s32[]{:S(2)}) async-start(), calls=%async_computation.1 | async-start | bytes 1572864 | tf_op jit(solution)/shard_map/all_gather | solution.py:56
  9.4 320.7 %all-reduce.4.cloned.1.call-start = ((), (), s32[]{:S(2)}) async-start(), calls=%async_computation.3 | async-start | bytes 442368 | tf_op jit(solution)/shard_map/psum | solution.py:98
  22.7 24.7 %collective-permute-start = (bf16[32,2,8,512]{3,0,2,1:T(8,128)(2,1)S(1)}, bf16[32,2,8,512]{3,0,2,1:T(8,128)(2,1)S(1)}, u32[]{:S(2)}, u32[]{:S(2)}) collective-permute-start(bf16[32,2,8,512]{3,0,2,1:T(8,128)(2,1)S(1)} %get-tuple-element.50), channel_id=1, source_target_pairs={{0,2},{2,4},{4,6},{6,8},{8,10},{10,12},{12,14},{14,0},{1,3},{3,5},... | collective-permute-start | bytes 1572872 | tf_op jit(solution)/shard_map/ppermute | solution.py:15
  24.5 25.1 %collective-permute-start.1 = (bf16[32,2,8,512]{3,0,2,1:T(8,128)(2,1)S(1)}, bf16[32,2,8,512]{3,0,2,1:T(8,128)(2,1)S(1)}, u32[]{:S(2)}, u32[]{:S(2)}) collective-permute-start(bf16[32,2,8,512]{3,0,2,1:T(8,128)(2,1)S(1)} %get-tuple-element.51), channel_id=1, source_target_pairs={{2,0},{4,2},{6,4},{8,6},{10,8},{12,10},{14,12},{0,14},{3,1},{5,3},... | collective-permute-start | bytes 1572872 | tf_op jit(solution)/shard_map/ppermute | solution.py:18
  99.2 7.7 %collective-permute-start.2 = (bf16[16,1,8,512]{3,0,2,1:T(8,128)(2,1)S(1)}, bf16[16,1,8,512]{3,0,2,1:T(8,128)(2,1)S(1)}, u32[]{:S(2)}, u32[]{:S(2)}) collective-permute-start(bf16[16,1,8,512]{3,0,2,1:T(8,128)(2,1)S(1)} %slice.824), channel_id=1, source_target_pairs={{14,0},{0,2},{2,4},{4,6},{6,8},{8,10},{10,12},{12,14},{15,1},{1,3}... | collective-permute-start | bytes 393224 | tf_op jit(solution)/shard_map/ppermute | solution.py:26
  127.9 22.3 %copy-start.41 = (bf16[16,2,4,1]{3,0,2,1:T(8,128)(2,1)S(1)}, bf16[16,2,4,1]{3,0,2,1:T(8,128)(2,1)}, u32[]{:S(2)}) copy-start(bf16[16,2,4,1]{3,0,2,1:T(8,128)(2,1)} %get-tuple-element.95) | copy-start | bytes 772
  136.3 31.7 %copy-start.40 = (bf16[16,2,4,1]{3,0,2,1:T(8,128)(2,1)S(1)}, bf16[16,2,4,1]{3,0,2,1:T(8,128)(2,1)}, u32[]{:S(2)}) copy-start(bf16[16,2,4,1]{3,0,2,1:T(8,128)(2,1)} %get-tuple-element.87) | copy-start | bytes 772
  143.1 40.0 %copy-start.39 = (bf16[16,2,4,1]{3,0,2,1:T(8,128)(2,1)S(1)}, bf16[16,2,4,1]{3,0,2,1:T(8,128)(2,1)}, u32[]{:S(2)}) copy-start(bf16[16,2,4,1]{3,0,2,1:T(8,128)(2,1)} %get-tuple-element.80) | copy-start | bytes 772
  143.8 44.7 %copy-start.37 = (bf16[16,2,4,1]{3,0,2,1:T(8,128)(2,1)S(1)}, bf16[16,2,4,1]{3,0,2,1:T(8,128)(2,1)}, u32[]{:S(2)}) copy-start(bf16[16,2,4,1]{3,0,2,1:T(8,128)(2,1)} %get-tuple-element.79) | copy-start | bytes 772
  146.3 47.7 %copy-start.38 = (bf16[16,2,4,1]{3,0,2,1:T(8,128)(2,1)S(1)}, bf16[16,2,4,1]{3,0,2,1:T(8,128)(2,1)}, u32[]{:S(2)}) copy-start(bf16[16,2,4,1]{3,0,2,1:T(8,128)(2,1)} %get-tuple-element.76) | copy-start | bytes 772
  150.2 49.1 %copy-start.36 = (bf16[16,2,4,1]{3,0,2,1:T(8,128)(2,1)S(1)}, bf16[16,2,4,1]{3,0,2,1:T(8,128)(2,1)}, u32[]{:S(2)}) copy-start(bf16[16,2,4,1]{3,0,2,1:T(8,128)(2,1)} %get-tuple-element.75) | copy-start | bytes 772
  157.6 52.6 %copy-start.35 = (bf16[16,2,4,1]{3,0,2,1:T(8,128)(2,1)S(1)}, bf16[16,2,4,1]{3,0,2,1:T(8,128)(2,1)}, u32[]{:S(2)}) copy-start(bf16[16,2,4,1]{3,0,2,1:T(8,128)(2,1)} %get-tuple-element.71) | copy-start | bytes 772
  188.5 50.1 %copy-start.8 = (bf16[16,2,4,256]{3,0,2,1:T(8,128)(2,1)S(1)}, bf16[16,2,4,256]{3,0,2,1:T(8,128)(2,1)}, u32[]{:S(2)}) copy-start(bf16[16,2,4,256]{3,0,2,1:T(8,128)(2,1)} %slice.685) | copy-start | bytes 196612
  201.0 40.8 %copy-start.7 = (bf16[16,2,4,256]{3,0,2,1:T(8,128)(2,1)S(1)}, bf16[16,2,4,256]{3,0,2,1:T(8,128)(2,1)}, u32[]{:S(2)}) copy-start(bf16[16,2,4,256]{3,0,2,1:T(8,128)(2,1)} %slice.696) | copy-start | bytes 196612
  211.8 33.2 %copy-start.6 = (bf16[16,2,4,256]{3,0,2,1:T(8,128)(2,1)S(1)}, bf16[16,2,4,256]{3,0,2,1:T(8,128)(2,1)}, u32[]{:S(2)}) copy-start(bf16[16,2,4,256]{3,0,2,1:T(8,128)(2,1)} %slice.707) | copy-start | bytes 196612
  236.9 9.7 %copy-start.18 = (bf16[16,2,4,256]{3,0,2,1:T(8,128)(2,1)S(1)}, bf16[16,2,4,256]{3,0,2,1:T(8,128)(2,1)}, u32[]{:S(2)}) copy-start(bf16[16,2,4,256]{3,0,2,1:T(8,128)(2,1)} %slice.716) | copy-start | bytes 196612
  236.9 12.1 %copy-start.20 = (bf16[16,2,4,256]{3,0,2,1:T(8,128)(2,1)S(1)}, bf16[16,2,4,256]{3,0,2,1:T(8,128)(2,1)}, u32[]{:S(2)}) copy-start(bf16[16,2,4,256]{3,0,2,1:T(8,128)(2,1)} %slice.727) | copy-start | bytes 196612
  239.3 11.2 %copy-start.9 = (bf16[16,2,4,256]{3,0,2,1:T(8,128)(2,1)S(1)}, bf16[16,2,4,256]{3,0,2,1:T(8,128)(2,1)}, u32[]{:S(2)}) copy-start(bf16[16,2,4,256]{3,0,2,1:T(8,128)(2,1)} %slice.733) | copy-start | bytes 196612
  240.1 11.2 %copy-start.22 = (bf16[16,2,4,256]{3,0,2,1:T(8,128)(2,1)S(1)}, bf16[16,2,4,256]{3,0,2,1:T(8,128)(2,1)}, u32[]{:S(2)}) copy-start(bf16[16,2,4,256]{3,0,2,1:T(8,128)(2,1)} %slice.738) | copy-start | bytes 196612
  242.6 10.3 %copy-start.11 = (bf16[16,2,4,256]{3,0,2,1:T(8,128)(2,1)S(1)}, bf16[16,2,4,256]{3,0,2,1:T(8,128)(2,1)}, u32[]{:S(2)}) copy-start(bf16[16,2,4,256]{3,0,2,1:T(8,128)(2,1)} %slice.744) | copy-start | bytes 196612
  243.4 10.3 %copy-start.24 = (bf16[16,2,4,256]{3,0,2,1:T(8,128)(2,1)S(1)}, bf16[16,2,4,256]{3,0,2,1:T(8,128)(2,1)}, u32[]{:S(2)}) copy-start(bf16[16,2,4,256]{3,0,2,1:T(8,128)(2,1)} %slice.749) | copy-start | bytes 196612
  248.9 9.4 %copy-start.28 = (bf16[16,2,4,256]{3,0,2,1:T(8,128)(2,1)S(1)}, bf16[16,2,4,256]{3,0,2,1:T(8,128)(2,1)}, u32[]{:S(2)}) copy-start(bf16[16,2,4,256]{3,0,2,1:T(8,128)(2,1)} %slice.771) | copy-start | bytes 196612
  260.8 78.7 %reduce-scatter.2.cloned.1.call-start = ((), (), s32[]{:S(2)}) async-start(), calls=%async_computation.2 | async-start | bytes 786432 | tf_op jit(solution)/shard_map/reduce_scatter | solution.py:96
  (24 other events, 97.3 us)
Sparse Core Ops, SparseCore 0:
  9.6 11.7 all-gather.1
  260.9 68.8 all-reduce.3
  332.2 7.2 reduce-scatter.1
where the time goes:
time: 354 us; the launch traced here: 348 us
  local copies, waits for them, and re-layouts  120 us (34%)
  matrix products  87.3 us (25%)
  waiting for transfers between devices  43.6 us (12%)
  blocking collectives  38.6 us (11%)
  other arithmetic  38.6 us (11%)
  between operations  14.9 us (4%)
  starting transfers between devices  5.22 us (1%)
    slice x45, local copies, waits for them, and re-layouts, take_taps(): return jnp.roll(selected, 1 - along_y, axis=3)[:, :, :, ::2]  101 us
    psum x1, blocking collectives, local(): lax.psum((jnp.stack(up_terms), jnp.stack(refine_terms)), ('gz', 'sec'))  36.5 us
    concatenate x18, other arithmetic, take_taps(): return jnp.roll(selected, 1 - along_y, axis=3)[:, :, :, ::2]  27.9 us
    dot_general x27, matrix products, local(): jnp.einsum('fc,fzxy->czxy', weight_block, selected, preferred_element_typ...  26.9 us
    dot_general x27, matrix products, local(): jnp.einsum('ozxy,czxy->oc', shifted, hidden, preferred_element_type=jnp.f...  25 us
    dot_general x27, matrix products, local(): jnp.einsum('czxy,fzxy->fc', all_coarse, selected, preferred_element_type=...  23.8 us
    ppermute x1, waiting for transfers between devices, padded(): lax.ppermute(lax.slice_in_dim(block, block.shape[dim] - width, None, axis...  18.3 us
    dot_general x27, matrix products, local(): jnp.einsum('oc,ozxy->czxy', refine_cols[tap_number], shifted, preferred_e...  11.6 us
  transfers between devices with their start and end apart: 6, of which 5 were waited for; matrix products, arithmetic and copies ran while one was open for 11% of the time, Pallas kernels for 0%

commit v1 on v0

--- a/solution.py
+++ b/solution.py
@@ -96,7 +96,7 @@
     coarse_summed = lax.psum_scatter(running, "ch", scatter_dimension=0, tiled=True)
     grad_coarse = coarse_summed.astype(jnp.bfloat16)
     up_summed, refine_summed = lax.psum(
-        (jnp.stack(up_terms), jnp.stack(refine_terms)), ("gz", "sec")
+        lax.psum((jnp.stack(up_terms), jnp.stack(refine_terms)), axis_name="sec"), axis_name="gz"
     )
     fine_total = planes_z * lax.axis_size("gz") * lax.axis_size("sec") * planes_x * cells_y
     coarse_total = fine_total // 8

time: 354 us -> 308 us (0.87)
  matrix products: 87.3 us -> 67 us
  local copies, waits for them, and re-layouts: 120 us -> 106 us
  blocking collectives: 38.6 us -> 33.5 us
  other arithmetic: 38.6 us -> 34.4 us
    dot_general x27, matrix products: 23.8 us -> 4.99 us  [local(): jnp.einsum('czxy,fzxy->fc', all_coarse, selected, preferred_element_type=...]
    slice x45, local copies, waits for them, and re-layouts: 101 us -> 86.3 us  [take_taps(): return jnp.roll(selected, 1 - along_y, axis=3)[:, :, :, ::2]]
    psum x1 -> x2, blocking collectives: 36.5 us -> 31.4 us  [the longest x1 22 us: local(): lax.psum(lax.psum((jnp.stack(up_terms), jnp.stack(refine_terms)), axis_na...]
    concatenate x18, other arithmetic: 27.9 us -> 23.6 us  [take_taps(): return jnp.roll(selected, 1 - along_y, axis=3)[:, :, :, ::2]]
  transfers between devices with their start and end apart: 6 -> 7, of which waited for: 5 -> 5; matrix products, arithmetic and copies ran while one was open for 11% -> 11% of each run, Pallas kernels for 0% -> 0%
where the time goes in v1:
time: 308 us; the launch traced here: 302 us
  local copies, waits for them, and re-layouts  106 us (34%)
  matrix products  67 us (22%)
  waiting for transfers between devices  41.5 us (13%)
  other arithmetic  34.4 us (11%)
  blocking collectives  33.5 us (11%)
  between operations  14.9 us (5%)
  starting transfers between devices  5.28 us (2%)
    slice x45, local copies, waits for them, and re-layouts, take_taps(): return jnp.roll(selected, 1 - along_y, axis=3)[:, :, :, ::2]  86.3 us
    dot_general x27, matrix products, local(): jnp.einsum('fc,fzxy->czxy', weight_block, selected, preferred_element_typ...  26.3 us
    dot_general x27, matrix products, local(): jnp.einsum('ozxy,czxy->oc', shifted, hidden, preferred_element_type=jnp.f...  24.1 us
    concatenate x18, other arithmetic, take_taps(): return jnp.roll(selected, 1 - along_y, axis=3)[:, :, :, ::2]  23.6 us
    psum x1, blocking collectives, local(): lax.psum(lax.psum((jnp.stack(up_terms), jnp.stack(refine_terms)), axis_na...  22 us
    ppermute x1, waiting for transfers between devices, padded(): lax.ppermute(lax.slice_in_dim(block, block.shape[dim] - width, None, axis...  18.3 us
    dot_general x27, matrix products, local(): jnp.einsum('oc,ozxy->czxy', refine_cols[tap_number], shifted, preferred_e...  11.6 us
    slice x8, local copies, waits for them, and re-layouts, local(): shifted = jnp.roll(shifted, 2 * (along_y - 1), axis=3)  10.1 us
  transfers between devices with their start and end apart: 7, of which 5 were waited for; matrix products, arithmetic and copies ran while one was open for 11% of the time, Pallas kernels for 0%

profile of v1, /device:TPU:0, one launch (start us, length us, event | category | flops | bytes accessed | tf_op | source)
XLA Modules:
  0.0 302.3 jit_solution(13494542343058815466)
XLA Ops:
  12.5 8.8 %all-gather.2.cloned.1.call-done = bf16[32,4,8,512]{3,0,2,1:T(8,128)(2,1)} async-done(((bf16[16,4,8,512]{3,0,2,1:T(8,128)(2,1)}), bf16[32,4,8,512]{3,0,2,1:T(8,128)(2,1)}) %all-gather.2.cloned.1.call-update) | async-done | bytes 1048592 | tf_op jit(solution)/shard_map/all_gather | solution.py:56
  24.5 3.0 collective-permute-start.1
  29.0 18.3 %collective-permute-done = bf16[32,2,8,512]{3,0,2,1:T(8,128)(2,1)S(1)} collective-permute-done((bf16[32,2,8,512]{3,0,2,1:T(8,128)(2,1)S(1)}, bf16[32,2,8,512]{3,0,2,1:T(8,128)(2,1)S(1)}, u32[]{:S(2)}, u32[]{:S(2)}) %collective-permute-start) | collective-permute-done | bytes 524320 | tf_op jit(solution)/shard_map/ppermute | solution.py:15
  50.0 4.9 %fusion.280 = (bf16[32,4,8,510]{3,0,2,1:T(8,128)(2,1)S(1)}, bf16[32,4,8,510]{3,0,2,1:T(8,128)(2,1)S(1)}, bf16[32,4,8,510]{3,0,2,1:T(8,128)(2,1)S(1)}, bf16[32,4,...) fusion(bf16[32,8,12,512]{3,0,2,1:T(8,128)(2,1)S(1)} %fusion.5), kind=kLoop, calls=%fused_computation.425 | loop fusion | bytes 25067520 | tf_op jit(solution)/shard_map/jit(_roll_static)/slice | solution.py:69
  102.5 6.5 %collective-permute-done.2 = bf16[16,1,8,512]{3,0,2,1:T(8,128)(2,1)S(1)} collective-permute-done((bf16[16,1,8,512]{3,0,2,1:T(8,128)(2,1)S(1)}, bf16[16,1,8,512]{3,0,2,1:T(8,128)(2,1)S(1)}, u32[]{:S(2)}, u32[]{:S(2)}) %collective-permute-start.2) | collective-permute-done | bytes 131104 | tf_op jit(solution)/shard_map/ppermute | solution.py:26
  110.6 2.7 slice.685
  152.7 2.5 slice.700
  156.9 3.2 %slice.705 = bf16[16,2,4,256]{3,0,2,1:T(8,128)(2,1)S(1)} slice(bf16[16,2,4,512]{3,0,2,1:T(8,128)(2,1)} %pad_maximum_fusion.22), slice={[0:16:1], [0:2:1], [0:4:1], [0:512:2]} | slice | bytes 131072 | tf_op jit(solution)/shard_map/slice | solution.py:42
  161.8 3.2 %slice.711 = bf16[16,2,4,256]{3,0,2,1:T(8,128)(2,1)S(1)} slice(bf16[16,2,4,512]{3,0,2,1:T(8,128)(2,1)} %pad_maximum_fusion.23), slice={[0:16:1], [0:2:1], [0:4:1], [0:512:2]} | slice | bytes 131072 | tf_op jit(solution)/shard_map/slice | solution.py:42
  166.6 3.2 %slice.716 = bf16[16,2,4,256]{3,0,2,1:T(8,128)(2,1)S(1)} slice(bf16[16,2,4,512]{3,0,2,1:T(8,128)(2,1)} %pad_maximum_fusion.24), slice={[0:16:1], [0:2:1], [0:4:1], [0:512:2]} | slice | bytes 131072 | tf_op jit(solution)/shard_map/slice | solution.py:42
  170.5 3.2 %slice.722 = bf16[16,2,4,256]{3,0,2,1:T(8,128)(2,1)S(1)} slice(bf16[16,2,4,512]{3,0,2,1:T(8,128)(2,1)} %pad_maximum_fusion.25), slice={[0:16:1], [0:2:1], [0:4:1], [0:512:2]} | slice | bytes 131072 | tf_op jit(solution)/shard_map/slice | solution.py:42
  175.4 3.2 %slice.727 = bf16[16,2,4,256]{3,0,2,1:T(8,128)(2,1)S(1)} slice(bf16[16,2,4,512]{3,0,2,1:T(8,128)(2,1)} %pad_maximum_fusion.26), slice={[0:16:1], [0:2:1], [0:4:1], [0:512:2]} | slice | bytes 131072 | tf_op jit(solution)/shard_map/slice | solution.py:42
  180.2 3.2 %slice.733 = bf16[16,2,4,256]{3,0,2,1:T(8,128)(2,1)S(1)} slice(bf16[16,2,4,512]{3,0,2,1:T(8,128)(2,1)} %pad_maximum_fusion.27), slice={[0:16:1], [0:2:1], [0:4:1], [0:512:2]} | slice | bytes 131072 | tf_op jit(solution)/shard_map/slice | solution.py:42
  185.0 3.2 %slice.738 = bf16[16,2,4,256]{3,0,2,1:T(8,128)(2,1)S(1)} slice(bf16[16,2,4,512]{3,0,2,1:T(8,128)(2,1)} %pad_maximum_fusion.28), slice={[0:16:1], [0:2:1], [0:4:1], [0:512:2]} | slice | bytes 131072 | tf_op jit(solution)/shard_map/slice | solution.py:42
  188.9 3.2 %slice.744 = bf16[16,2,4,256]{3,0,2,1:T(8,128)(2,1)S(1)} slice(bf16[16,2,4,512]{3,0,2,1:T(8,128)(2,1)} %pad_maximum_fusion.29), slice={[0:16:1], [0:2:1], [0:4:1], [0:512:2]} | slice | bytes 131072 | tf_op jit(solution)/shard_map/slice | solution.py:42
  193.8 3.2 %slice.749 = bf16[16,2,4,256]{3,0,2,1:T(8,128)(2,1)S(1)} slice(bf16[16,2,4,512]{3,0,2,1:T(8,128)(2,1)} %pad_maximum_fusion.30), slice={[0:16:1], [0:2:1], [0:4:1], [0:512:2]} | slice | bytes 131072 | tf_op jit(solution)/shard_map/slice | solution.py:42
  198.6 3.2 %slice.755 = bf16[16,2,4,256]{3,0,2,1:T(8,128)(2,1)S(1)} slice(bf16[16,2,4,512]{3,0,2,1:T(8,128)(2,1)} %pad_maximum_fusion.31), slice={[0:16:1], [0:2:1], [0:4:1], [0:512:2]} | slice | bytes 131072 | tf_op jit(solution)/shard_map/slice | solution.py:42
  203.4 3.2 %slice.760 = bf16[16,2,4,256]{3,0,2,1:T(8,128)(2,1)S(1)} slice(bf16[16,2,4,512]{3,0,2,1:T(8,128)(2,1)} %pad_maximum_fusion.32), slice={[0:16:1], [0:2:1], [0:4:1], [0:512:2]} | slice | bytes 131072 | tf_op jit(solution)/shard_map/slice | solution.py:42
  207.4 3.4 %slice.766 = bf16[16,2,4,256]{3,0,2,1:T(8,128)(2,1)S(1)} slice(bf16[16,2,4,512]{3,0,2,1:T(8,128)(2,1)} %pad_maximum_fusion.33), slice={[0:16:1], [0:2:1], [0:4:1], [0:512:2]} | slice | bytes 131072 | tf_op jit(solution)/shard_map/slice | solution.py:42
  212.4 3.2 %slice.771 = bf16[16,2,4,256]{3,0,2,1:T(8,128)(2,1)S(1)} slice(bf16[16,2,4,512]{3,0,2,1:T(8,128)(2,1)} %pad_maximum_fusion.34), slice={[0:16:1], [0:2:1], [0:4:1], [0:512:2]} | slice | bytes 131072 | tf_op jit(solution)/shard_map/slice | solution.py:42
  216.3 3.2 %slice.777 = bf16[16,2,4,256]{3,0,2,1:T(8,128)(2,1)S(1)} slice(bf16[16,2,4,512]{3,0,2,1:T(8,128)(2,1)} %pad_maximum_fusion.35), slice={[0:16:1], [0:2:1], [0:4:1], [0:512:2]} | slice | bytes 131072 | tf_op jit(solution)/shard_map/slice | solution.py:42
  254.5 9.5 %psum.30 = f32[27,32,16]{1,2,0:T(8,128)S(1)} all-reduce(f32[27,32,16]{1,2,0:T(8,128)S(1)} %fusion.16), channel_id=1, replica_groups=mesh['groups'=2,'gz'=4,'sec'=2,'ch'=2] {'sec'}, use_global_device_ids=true, to_apply=%region_3.4 | all-reduce | flops 13824 | bytes 110592 | tf_op jit(solution)/shard_map/psum | solution.py:99
  264.0 22.0 %psum.31 = f32[27,32,16]{1,2,0:T(8,128)S(1)} all-reduce(f32[27,32,16]{1,2,0:T(8,128)S(1)} %psum.30), channel_id=1, replica_groups=mesh['groups'=2,'gz'=4,'sec'=2,'ch'=2] {'gz'}, use_global_device_ids=true, to_apply=%region_4.5 | all-reduce | flops 13824 | bytes 110592 | tf_op jit(solution)/shard_map/psum | solution.py:98
  288.3 5.5 %reduce-scatter.2.cloned.1.call-done = f32[32,2,4,256]{3,0,2,1:T(8,128)} async-done(((f32[64,2,4,256]{3,0,2,1:T(8,128)}), f32[32,2,4,256]{3,0,2,1:T(8,128)}) %reduce-scatter.2.cloned.1.call-update) | async-done | bytes 262160 | tf_op jit(solution)/shard_map/reduce_scatter | solution.py:96
  (249 shorter events, 159.1 us)
Async XLA Ops:
  7.2 80.6 %copy-start = (bf16[27,32,32]{2,1,0:T(8,128)(2,1)S(1)}, bf16[27,32,32]{2,1,0:T(8,128)(2,1)}, u32[]{:S(2)}) copy-start(bf16[27,32,32]{2,1,0:T(8,128)(2,1)} %param.9) | copy-start | bytes 165892
  7.2 14.1 %all-gather.2.cloned.1.call-start = ((), (), s32[]{:S(2)}) async-start(), calls=%async_computation.1 | async-start | bytes 1572864 | tf_op jit(solution)/shard_map/all_gather | solution.py:56
  9.4 240.5 %all-reduce.5.cloned.1.call-start = ((), (), s32[]{:S(2)}) async-start(), calls=%async_computation.3 | async-start | bytes 442368 | tf_op jit(solution)/shard_map/psum | solution.py:99
  21.3 6.1 %copy-start.1 = (bf16[32,4,8,512]{3,0,2,1:T(8,128)(2,1)S(1)}, bf16[32,4,8,512]{3,0,2,1:T(8,128)(2,1)}, u32[]{:S(2)}) copy-start(bf16[32,4,8,512]{3,0,2,1:T(8,128)(2,1)} %all-gather.2.cloned.1.call-done) | copy-start | bytes 3145732
  22.7 24.7 %collective-permute-start = (bf16[32,2,8,512]{3,0,2,1:T(8,128)(2,1)S(1)}, bf16[32,2,8,512]{3,0,2,1:T(8,128)(2,1)S(1)}, u32[]{:S(2)}, u32[]{:S(2)}) collective-permute-start(bf16[32,2,8,512]{3,0,2,1:T(8,128)(2,1)S(1)} %get-tuple-element.50), channel_id=1, source_target_pairs={{0,2},{2,4},{4,6},{6,8},{8,10},{10,12},{12,14},{14,0},{1,3},{3,5},... | collective-permute-start | bytes 1572872 | tf_op jit(solution)/shard_map/ppermute | solution.py:15
  24.5 25.1 %collective-permute-start.1 = (bf16[32,2,8,512]{3,0,2,1:T(8,128)(2,1)S(1)}, bf16[32,2,8,512]{3,0,2,1:T(8,128)(2,1)S(1)}, u32[]{:S(2)}, u32[]{:S(2)}) collective-permute-start(bf16[32,2,8,512]{3,0,2,1:T(8,128)(2,1)S(1)} %get-tuple-element.51), channel_id=1, source_target_pairs={{2,0},{4,2},{6,4},{8,6},{10,8},{12,10},{14,12},{0,14},{3,1},{5,3},... | collective-permute-start | bytes 1572872 | tf_op jit(solution)/shard_map/ppermute | solution.py:18
  59.9 1.0 copy-start.11
  60.9 1.0 copy-start.14
  66.9 1.0 copy-start.9
  70.4 1.0 copy-start.7
  77.0 1.0 copy-start.5
  101.3 7.7 %collective-permute-start.2 = (bf16[16,1,8,512]{3,0,2,1:T(8,128)(2,1)S(1)}, bf16[16,1,8,512]{3,0,2,1:T(8,128)(2,1)S(1)}, u32[]{:S(2)}, u32[]{:S(2)}) collective-permute-start(bf16[16,1,8,512]{3,0,2,1:T(8,128)(2,1)S(1)} %slice.824), channel_id=1, source_target_pairs={{14,0},{0,2},{2,4},{4,6},{6,8},{8,10},{10,12},{12,14},{15,1},{1,3}... | collective-permute-start | bytes 393224 | tf_op jit(solution)/shard_map/ppermute | solution.py:26
  102.5 7.5 %copy-start.17 = (f32[27,32,16]{1,2,0:T(8,128)}, f32[27,32,16]{1,2,0:T(8,128)S(1)}, u32[]{:S(2)}) copy-start(f32[27,32,16]{1,2,0:T(8,128)S(1)} %fusion.18) | copy-start | bytes 165892
  127.8 23.9 %copy-start.23 = (bf16[16,2,4,1]{3,0,2,1:T(8,128)(2,1)S(1)}, bf16[16,2,4,1]{3,0,2,1:T(8,128)(2,1)}, u32[]{:S(2)}) copy-start(bf16[16,2,4,1]{3,0,2,1:T(8,128)(2,1)} %get-tuple-element.91) | copy-start | bytes 772
  128.6 26.7 %copy-start.24 = (bf16[16,2,4,1]{3,0,2,1:T(8,128)(2,1)S(1)}, bf16[16,2,4,1]{3,0,2,1:T(8,128)(2,1)}, u32[]{:S(2)}) copy-start(bf16[16,2,4,1]{3,0,2,1:T(8,128)(2,1)} %get-tuple-element.88) | copy-start | bytes 772
  131.7 28.4 %copy-start.21 = (bf16[16,2,4,1]{3,0,2,1:T(8,128)(2,1)S(1)}, bf16[16,2,4,1]{3,0,2,1:T(8,128)(2,1)}, u32[]{:S(2)}) copy-start(bf16[16,2,4,1]{3,0,2,1:T(8,128)(2,1)} %get-tuple-element.87) | copy-start | bytes 772
  134.7 30.2 %copy-start.22 = (bf16[16,2,4,1]{3,0,2,1:T(8,128)(2,1)S(1)}, bf16[16,2,4,1]{3,0,2,1:T(8,128)(2,1)}, u32[]{:S(2)}) copy-start(bf16[16,2,4,1]{3,0,2,1:T(8,128)(2,1)} %get-tuple-element.84) | copy-start | bytes 772
  148.3 43.8 %copy-start.20 = (bf16[16,2,4,1]{3,0,2,1:T(8,128)(2,1)S(1)}, bf16[16,2,4,1]{3,0,2,1:T(8,128)(2,1)}, u32[]{:S(2)}) copy-start(bf16[16,2,4,1]{3,0,2,1:T(8,128)(2,1)} %get-tuple-element.72) | copy-start | bytes 772
  155.3 46.5 %copy-start.19 = (bf16[16,2,4,1]{3,0,2,1:T(8,128)(2,1)S(1)}, bf16[16,2,4,1]{3,0,2,1:T(8,128)(2,1)}, u32[]{:S(2)}) copy-start(bf16[16,2,4,1]{3,0,2,1:T(8,128)(2,1)} %get-tuple-element.68) | copy-start | bytes 772
  225.2 61.5 %all-reduce.7.cloned.1.call-start = ((), (), s32[]{:S(2)}) async-start(), calls=%async_computation.4 | async-start | bytes 442368 | tf_op jit(solution)/shard_map/psum | solution.py:98
  247.9 3.9 %copy-start.2 = (bf16[32,4,8,512]{3,0,2,1:T(8,128)(2,1)S(1)}, bf16[32,4,8,512]{3,0,2,1:T(8,128)(2,1)}, u32[]{:S(2)}) copy-start(bf16[32,4,8,512]{3,0,2,1:T(8,128)(2,1)} %get-tuple-element.6) | copy-start | bytes 3145732
  247.9 3.9 %copy-start.18 = (f32[27,32,16]{1,2,0:T(8,128)S(1)}, f32[27,32,16]{1,2,0:T(8,128)}, u32[]{:S(2)}) copy-start(f32[27,32,16]{1,2,0:T(8,128)} %copy-done.17) | copy-start | bytes 165892
  250.0 43.9 %reduce-scatter.2.cloned.1.call-start = ((), (), s32[]{:S(2)}) async-start(), calls=%async_computation.2 | async-start | bytes 786432 | tf_op jit(solution)/shard_map/reduce_scatter | solution.py:96
  251.8 1.9 copy-start.15
  (8 other events, 7.4 us)
Sparse Core Ops, SparseCore 0:
  9.6 11.7 all-gather.1
  225.3 20.9 all-reduce.4
  250.1 34.1 all-reduce.6
  286.5 7.3 reduce-scatter.1
